TPU v7x, 256 devices: a whole 4x4x8 slice. The times are simulated.
256 devices in a mesh: graph: 8 (over z), index: 32 (over x, y, core).
Axes of the slice: x: 4, y: 4, z: 8, core: 2. Of those that a mesh axis runs over, the one named last changes fastest.
Arguments:
- features: bfloat16 [65536, 1024], P(('graph', 'index')), may hold values from -6 to 6
- q_weight: bfloat16 [1024, 1024], replicated, may hold values from -0.1875 to 0.1875
- q_bias: float32 [1024], replicated, may hold values from -3 to 3
- w_self: bfloat16 [1024, 1024], replicated, may hold values from -0.125 to 0.125
- w_neigh: bfloat16 [1024, 1024], replicated, may hold values from -0.125 to 0.125
- z_bias: float32 [1024], replicated, may hold values from -3 to 3
- centroids: bfloat16 [8192, 1024], P('index'), may hold values from -0.1875 to 0.1875
- requests: int32 [256, 32, 16], P(('graph', 'index')), may hold values from 0 to 255, as said below
- slots: int32 [65536, 50], P(('graph', 'index')), may hold values from 0 to 511
- importance: float32 [65536, 50], P(('graph', 'index')), may hold values from 0.1 to 10
- labels: int32 [65536, 1], P(('graph', 'index')), may hold values from 0 to 31; in each aligned block of 256 rows (0 to 255, 256 to 511, ...) at most 16 rows name the same one
Outputs:
- scores: bfloat16 [65536, 256], P(('graph', 'index'))
Inputs may be any that keep to these rules, and one draw needn't show every extreme that they name: `requests`: the 16 rows that a device asks of one device are distinct. `labels`: the rows of one device carry any one label at most 16 times.
All inputs are finite; a program needn't handle non-finite values.
Results may differ from a plain program's by a relative error of at most 0.0051.
Values may be sent and summed in bfloat16 or wider, within the bound.
No kernel may reach another device: no remote copies, remote signals or barrier semaphores. Data moves between devices by JAX's collectives and lax.ppermute only.
A program may use at most 64 MiB of HBM per device.

v0:
```python
import jax
import jax.numpy as jnp
from jax import lax
from jax.sharding import PartitionSpec as P


def place_rows(label_rows, peer_count, owner_slots):
    hits = (label_rows[:, None] == jnp.arange(peer_count, dtype=jnp.int32)[None, :]).astype(
        jnp.int32
    )
    ranks = jnp.sum(hits * (jnp.cumsum(hits, axis=0) - 1), axis=1)
    return label_rows * owner_slots + ranks


def one_hot(index, count):
    return (index[:, None] == jnp.arange(count, dtype=jnp.int32)[None, :]).astype(jnp.bfloat16)


def body(
    features,
    q_weight,
    q_bias,
    w_self,
    w_neigh,
    z_bias,
    centroids,
    requests,
    slots,
    importance,
    labels,
):
    row_count = features.shape[0]
    width = features.shape[1]
    peer_count = lax.axis_size("index")
    owner_slots = max(2 * row_count // peer_count, 2)
    fetch_slots = requests.shape[2]
    slot_count = peer_count * fetch_slots
    cent_count = centroids.shape[0]
    me = lax.axis_index("index")
    own_rows = jnp.where(
        jnp.arange(peer_count, dtype=jnp.int32)[:, None, None] == me,
        requests.astype(jnp.float32),
        0.0,
    )
    all_requests = lax.psum(own_rows, "index")
    wanted = lax.dynamic_index_in_dim(all_requests, me, axis=1, keepdims=False).astype(jnp.int32)
    messages = jax.nn.relu(
        jnp.dot(features, q_weight, preferred_element_type=jnp.float32) + q_bias
    ).astype(jnp.bfloat16)
    weights_norm = importance / jnp.sum(importance, axis=1, keepdims=True)
    slot_ids = jnp.arange(slot_count, dtype=jnp.int32)
    mixing = jnp.sum(
        jnp.where(slots[:, :, None] == slot_ids[None, None, :], weights_norm[:, :, None], 0.0),
        axis=1,
    ).astype(jnp.bfloat16)
    outgoing_msgs = jnp.dot(
        one_hot(wanted.reshape(-1), row_count),
        lax.optimization_barrier(messages),
        preferred_element_type=jnp.float32,
    ).astype(jnp.bfloat16)
    fetched = lax.all_to_all(
        outgoing_msgs.reshape(peer_count, fetch_slots, width),
        "index",
        split_axis=0,
        concat_axis=0,
        tiled=True,
    ).reshape(slot_count, width)
    pooled = jnp.dot(mixing, fetched, preferred_element_type=jnp.float32).astype(jnp.bfloat16)
    hidden = jax.nn.relu(
        jnp.dot(features, w_self, preferred_element_type=jnp.float32)
        + jnp.dot(pooled, w_neigh, preferred_element_type=jnp.float32)
        + z_bias
    )
    normed = (hidden * lax.rsqrt(jnp.mean(hidden * hidden, axis=1, keepdims=True) + 1e-06)).astype(
        jnp.bfloat16
    )
    positions = place_rows(labels[:, 0], peer_count, owner_slots)
    pick = one_hot(positions, peer_count * owner_slots)
    outgoing = lax.dot_general(
        pick, normed, (((0,), (0,)), ((), ())), preferred_element_type=jnp.float32
    ).astype(jnp.bfloat16)
    outgoing = outgoing.reshape(peer_count, owner_slots, width)
    arrived = lax.all_to_all(outgoing, "index", split_axis=0, concat_axis=0, tiled=True)
    flat_rows = arrived.reshape(-1, width)
    raw_scores = lax.dot_general(
        flat_rows, centroids, (((1,), (1,)), ((), ())), preferred_element_type=jnp.float32
    ).astype(jnp.bfloat16)
    returned = lax.all_to_all(
        raw_scores.reshape(peer_count, arrived.shape[1], cent_count),
        "index",
        split_axis=0,
        concat_axis=0,
        tiled=True,
    )
    return jnp.dot(
        pick,
        returned.reshape(peer_count * owner_slots, cent_count),
        preferred_element_type=jnp.float32,
    ).astype(jnp.bfloat16)


def solution(mesh):
    return jax.shard_map(
        body,
        mesh=mesh,
        in_specs=(
            P(("graph", "index"), None),
            P(),
            P(),
            P(),
            P(),
            P(),
            P("index", None),
            P(("graph", "index"), None, None),
            P(("graph", "index"), None),
            P(("graph", "index"), None),
            P(("graph", "index"), None),
        ),
        out_specs=P(("graph", "index"), None),
        check_vma=False,
    )
```

profile of v0, /device:TPU:1, one launch (start us, length us, event | category | flops | bytes accessed | tf_op | source)
XLA Modules:
  0.0 201.9 jit_solution(17790053467064373194)
XLA Ops:
  6.5 0.0 copy-start
  6.5 0.0 all-reduce.2.cloned.1.call-start
  6.5 0.8 convert_bitcast_fusion
  7.4 0.1 copy.20
  7.5 0.9 broadcast_select_fusion
  8.4 0.0 copy-start.6
  8.4 0.0 all-reduce.2.cloned.1.call-update
  8.4 0.7 fusion.12
  9.1 0.6 reduce-window.6
  9.7 0.2 slice_reduce_fusion
  9.9 0.0 copy-start.4
  9.9 2.6 %fusion.13 = f32[256,1024]{1,0:T(8,128)S(1)} fusion(bf16[256,1024]{1,0:T(8,128)(2,1)} %param.11, bf16[1024,1024]{1,0:T(8,128)(2,1)} %param.14), kind=kOutput, calls=%fused_computation.37 | convolution fusion | flops 536870912 | bytes 3670016 | tf_op jit(solution)/shard_map/dot_general | solution.py:70
  12.6 0.0 copy-done.6
  12.6 0.0 copy-done.4
  12.6 0.0 copy-start.3
  12.6 2.6 %fusion.3 = bf16[256,1024]{1,0:T(8,128)(2,1)} fusion(bf16[256,1024]{1,0:T(8,128)(2,1)} %param.11, bf16[1024,1024]{1,0:T(8,128)(2,1)S(1)} %copy-done.4, f32[1024]{0:T(1024)S(1)} %copy-done.6), kind=kOutput, calls=%fused_computation.9 | convolution fusion | flops 537657344 | bytes 3149824 | tf_op jit(solution)/shard_map/dot_general | solution.py:48
  15.1 0.0 copy-start.1
  15.1 0.0 copy-start.2
  15.1 0.0 copy-done.3
  15.1 0.1 fusion.11
  15.2 113.5 %all-reduce.2.cloned.1.call-done = f32[32,32,16]{2,0,1:T(8,128)} async-done(((f32[32,32,16]{2,0,1:T(8,128)}), f32[32,32,16]{2,0,1:T(8,128)}) %all-reduce.2.cloned.1.call-update) | async-done | bytes 65552 | tf_op jit(solution)/shard_map/psum | solution.py:45
  128.7 0.7 dynamic-slice_convert_fusion
  129.4 0.1 convert_element_type.48
  129.5 0.0 copy-start.7
  129.5 2.6 %convolution_convert_fusion.1 = bf16[512,1024]{1,0:T(8,128)(2,1)} fusion(bf16[256,1024]{1,0:T(8,128)(2,1)} %fusion.3, s32[512]{0:T(512)S(1)} %convert_element_type.48), kind=kOutput, calls=%fused_computation.3 | convolution fusion | flops 269090816 | bytes 1574912 | tf_op jit(solution)/shard_map/dot_general | solution.py:56
  132.1 6.1 %all-to-all-start = ((bf16[32,16,1024]{2,1,0:T(8,128)(2,1)}), bf16[32,16,1024]{2,1,0:T(8,128)(2,1)}, u32[]{:S(2)}, u32[]{:S(2)}) async-start(bf16[32,16,1024]{2,1,0:T(8,128)(2,1)} %bitcast.6), calls=%async_computation | async-start | bytes 2097152 | tf_op jit(solution)/shard_map/all_to_all | solution.py:61
  138.2 0.0 copy-done.1
  138.3 0.0 copy-done.2
  138.3 4.3 %select_reduce_fusion = bf16[256,512]{1,0:T(8,128)(2,1)S(1)} fusion(f32[256,50]{0,1:T(8,128)S(1)} %broadcast_divide_fusion, s32[256,50]{0,1:T(8,128)S(1)} %copy-done.2), kind=kLoop, calls=%fused_computation | loop fusion | flops 19529728 | bytes 364544 | tf_op jit(solution)/shard_map/reduce_sum | solution.py:52
  142.6 12.5 %all-to-all-done = bf16[32,16,1024]{2,1,0:T(8,128)(2,1)} async-done(((bf16[32,16,1024]{2,1,0:T(8,128)(2,1)}), bf16[32,16,1024]{2,1,0:T(8,128)(2,1)}, u32[]{:S(2)}, u32[]{:S(2)}) %all-to-all-start) | async-done | bytes 1048608 | tf_op jit(solution)/shard_map/all_to_all | solution.py:61
  155.1 0.0 copy-done
  155.1 0.0 copy-done.7
  155.2 3.3 %multiply_reduce_fusion = (f32[256]{0:T(256)S(1)}, f32[256,1024]{1,0:T(8,128)}) fusion(f32[1024]{0:T(1024)S(1)} %copy-done.7, f32[256,1024]{1,0:T(8,128)S(1)} %fusion.13, bf16[1024,1024]{1,0:T(8,128)(2,1)S(1)} %copy-done, bf16[512,1024]{1,0:T(8,128)(2,1)} %bitcast.7, bf16[256,512]{1,0:T(8,128)(2,1)S(1)} %select_reduce_fusion), kind=kOutput, calls=%fused_computation.14 | convolution fusion | flops 806878976 | bytes 5510144 | tf_op jit(solution)/shard_map/dot_general | solution.py:71
  158.4 0.0 copy-start.5
  158.4 1.8 convolution_convert_fusion
  160.3 20.6 %all_to_all.15 = bf16[32,16,1024]{2,1,0:T(8,128)(2,1)S(1)} all-to-all(bf16[32,16,1024]{2,1,0:T(8,128)(2,1)S(1)} %bitcast.40), channel_id=1, replica_groups=mesh['graph'=8,'index'=32] {'index'}, dimensions={0} | all-to-all | bytes 2097152 | tf_op jit(solution)/shard_map/all_to_all | solution.py:83
  180.9 0.0 copy-done.5
  180.9 0.5 convolution_convert_fusion.3
  181.4 12.7 %all_to_all.16 = bf16[32,16,256]{2,1,0:T(8,128)(2,1)S(1)} all-to-all(bf16[32,16,256]{2,1,0:T(8,128)(2,1)S(1)} %bitcast.43), channel_id=1, replica_groups=mesh['graph'=8,'index'=32] {'index'}, dimensions={0} | all-to-all | bytes 524288 | tf_op jit(solution)/shard_map/all_to_all | solution.py:88
  194.1 0.9 convolution_convert_fusion.4
  (7 shorter events, 0.1 us)
Async XLA Ops:
  6.5 148.6 %copy-start = (bf16[1024,1024]{1,0:T(8,128)(2,1)S(1)}, bf16[1024,1024]{1,0:T(8,128)(2,1)}, u32[]{:S(2)}) copy-start(bf16[1024,1024]{1,0:T(8,128)(2,1)} %param.15) | copy-start | bytes 6291460
  6.5 122.2 %all-reduce.2.cloned.1.call-start = ((), (), s32[]{:S(2)}) async-start(), calls=%async_computation.3 | async-start | bytes 1048576 | tf_op jit(solution)/shard_map/psum | solution.py:45
  8.4 4.1 %copy-start.6 = (f32[1024]{0:T(1024)S(1)}, f32[1024]{0:T(1024)}, u32[]{:S(2)}) copy-start(f32[1024]{0:T(1024)} %param.13) | copy-start | bytes 12292
  9.9 2.6 %copy-start.4 = (bf16[1024,1024]{1,0:T(8,128)(2,1)S(1)}, bf16[1024,1024]{1,0:T(8,128)(2,1)}, u32[]{:S(2)}) copy-start(bf16[1024,1024]{1,0:T(8,128)(2,1)} %param.12) | copy-start | bytes 6291460
  12.6 2.6 %copy-start.3 = (s32[256,1]{0,1:T(1,128)S(1)}, s32[256,1]{0,1:T(1,128)}, u32[]{:S(2)}) copy-start(s32[256,1]{0,1:T(1,128)} %param.21) | copy-start | bytes 3076
  15.1 123.1 %copy-start.1 = (f32[256,50]{0,1:T(8,128)S(1)}, f32[256,50]{0,1:T(8,128)}, u32[]{:S(2)}) copy-start(f32[256,50]{0,1:T(8,128)} %param.20) | copy-start | bytes 153604
  15.1 123.1 %copy-start.2 = (s32[256,50]{0,1:T(8,128)S(1)}, s32[256,50]{0,1:T(8,128)}, u32[]{:S(2)}) copy-start(s32[256,50]{0,1:T(8,128)} %param.19) | copy-start | bytes 153604
  129.5 25.6 %copy-start.7 = (f32[1024]{0:T(1024)S(1)}, f32[1024]{0:T(1024)}, u32[]{:S(2)}) copy-start(f32[1024]{0:T(1024)} %param.16) | copy-start | bytes 12292
  132.1 23.0 %all-to-all-start = ((bf16[32,16,1024]{2,1,0:T(8,128)(2,1)}), bf16[32,16,1024]{2,1,0:T(8,128)(2,1)}, u32[]{:S(2)}, u32[]{:S(2)}) async-start(bf16[32,16,1024]{2,1,0:T(8,128)(2,1)} %bitcast.6), calls=%async_computation | async-start | bytes 2097152 | tf_op jit(solution)/shard_map/all_to_all | solution.py:61
  158.4 22.5 %copy-start.5 = (bf16[256,1024]{1,0:T(8,128)(2,1)S(1)}, bf16[256,1024]{1,0:T(8,128)(2,1)}, u32[]{:S(2)}) copy-start(bf16[256,1024]{1,0:T(8,128)(2,1)} %param.17) | copy-start | bytes 1572868
Sparse Core Ops, SparseCore 0:
  10.5 118.1 all-reduce.1
where the time goes:
time: 202 us
  waiting for transfers between devices  126 us (62%)
  blocking collectives  33.3 us (16%)
  matrix products  14.3 us (7%)
  between operations  13.5 us (7%)
  other arithmetic  8.31 us (4%)
  starting transfers between devices  6.08 us (3%)
    psum x1, waiting for transfers between devices, body(): all_requests = lax.psum(own_rows, 'index')  113 us
    all_to_all x1, blocking collectives, body(): lax.all_to_all(outgoing, 'index', split_axis=0, concat_axis=0, tiled=True)  20.6 us
    all_to_all x1, blocking collectives, body(): lax.all_to_all(raw_scores.reshape(peer_count, arrived.shape[1], cent_coun...  12.7 us
    all_to_all x1, waiting for transfers between devices, body(): lax.all_to_all(outgoing_msgs.reshape(peer_count, fetch_slots, width), 'in...  12.5 us
    all_to_all x1, starting transfers between devices, body(): lax.all_to_all(outgoing_msgs.reshape(peer_count, fetch_slots, width), 'in...  6.08 us
    reduce_sum x1, other arithmetic, body(): jnp.sum(jnp.where(slots[:, :, None] == slot_ids[None, None, :], weights_n...  4.35 us
  transfers between devices with their start and end apart: 2, of which 2 were waited for; matrix products, arithmetic and copies ran while one was open for 6% of the time, Pallas kernels for 0%

commit v1 on v0

--- a/solution.py
+++ b/solution.py
@@ -42,7 +42,7 @@
         requests.astype(jnp.float32),
         0.0,
     )
-    all_requests = lax.psum(own_rows, "index")
+    all_requests = jnp.sum(lax.all_gather(own_rows, "index"), axis=0)
     wanted = lax.dynamic_index_in_dim(all_requests, me, axis=1, keepdims=False).astype(jnp.int32)
     messages = jax.nn.relu(
         jnp.dot(features, q_weight, preferred_element_type=jnp.float32) + q_bias

time: 202 us -> 149 us (0.74)
  waiting for transfers between devices: 126 us -> 69.5 us
  other arithmetic: 8.31 us -> 11.6 us
    psum x1 -> x0, waiting for transfers between devices: 113 us -> none  [body(): all_requests = lax.psum(own_rows, 'index')]
    all_gather x0 -> x1, waiting for transfers between devices: none -> 57 us  [body(): all_requests = jnp.sum(lax.all_gather(own_rows, 'index'), axis=0)]
    reduce_sum x0 -> x1, other arithmetic: none -> 4.04 us  [body(): all_requests = jnp.sum(lax.all_gather(own_rows, 'index'), axis=0)]
  transfers between devices with their start and end apart: 2 -> 2, of which waited for: 2 -> 2; matrix products, arithmetic and copies ran while one was open for 6% -> 7% of each run, Pallas kernels for 0% -> 0%
where the time goes in v1:
time: 149 us
  waiting for transfers between devices  69.5 us (47%)
  blocking collectives  33.3 us (22%)
  matrix products  14.8 us (10%)
  between operations  13.5 us (9%)
  other arithmetic  11.6 us (8%)
  starting transfers between devices  5.54 us (4%)
    all_gather x1, waiting for transfers between devices, body(): all_requests = jnp.sum(lax.all_gather(own_rows, 'index'), axis=0)  57 us
    all_to_all x1, blocking collectives, body(): lax.all_to_all(outgoing, 'index', split_axis=0, concat_axis=0, tiled=True)  20.6 us
    all_to_all x1, blocking collectives, body(): lax.all_to_all(raw_scores.reshape(peer_count, arrived.shape[1], cent_coun...  12.7 us
    all_to_all x1, waiting for transfers between devices, body(): lax.all_to_all(outgoing_msgs.reshape(peer_count, fetch_slots, width), 'in...  12.5 us
    all_to_all x1, starting transfers between devices, body(): lax.all_to_all(outgoing_msgs.reshape(peer_count, fetch_slots, width), 'in...  5.54 us
    reduce_sum x1, other arithmetic, body(): jnp.sum(jnp.where(slots[:, :, None] == slot_ids[None, None, :], weights_n...  4.35 us
    reduce_sum x1, other arithmetic, body(): all_requests = jnp.sum(lax.all_gather(own_rows, 'index'), axis=0)  4.04 us
    dot_general x1, matrix products, body(): jnp.dot(pooled, w_neigh, preferred_element_type=jnp.float32)  3.27 us
  transfers between devices with their start and end apart: 2, of which 2 were waited for; matrix products, arithmetic and copies ran while one was open for 7% of the time, Pallas kernels for 0%

profile of v1, /device:TPU:1, one launch (start us, length us, event | category | flops | bytes accessed | tf_op | source)
XLA Modules:
  0.0 148.6 jit_solution(885160135929034312)
XLA Ops:
  6.5 0.0 copy-start
  6.5 0.0 all-gather.2.cloned.1.call-start
  6.5 0.8 convert_bitcast_fusion
  7.4 0.8 broadcast_select_fusion
  8.2 0.0 copy-start.3
  8.2 0.0 all-gather.2.cloned.1.call-update
  8.3 3.2 %fusion.3 = bf16[256,1024]{1,0:T(8,128)(2,1)} fusion(bf16[256,1024]{1,0:T(8,128)(2,1)} %param.11, bf16[1024,1024]{1,0:T(8,128)(2,1)} %param.12, f32[1024]{0:T(1024)} %param.13), kind=kOutput, calls=%fused_computation.9 | convolution fusion | flops 537657344 | bytes 3149824 | tf_op jit(solution)/shard_map/dot_general | solution.py:48
  11.5 0.0 copy-done.3
  11.5 0.6 reduce-window.6
  12.1 0.2 slice_reduce_fusion
  12.3 0.1 fusion.11
  12.4 2.5 %fusion.13 = f32[256,1024]{1,0:T(8,128)S(1)} fusion(bf16[256,1024]{1,0:T(8,128)(2,1)} %param.11, bf16[1024,1024]{1,0:T(8,128)(2,1)} %param.14), kind=kOutput, calls=%fused_computation.37 | convolution fusion | flops 536870912 | bytes 3670016 | tf_op jit(solution)/shard_map/dot_general | solution.py:70
  14.9 57.0 %all-gather.2.cloned.1.call-done = f32[32,32,32,16]{2,3,1,0:T(8,128)} async-done(((f32[1,32,32,16]{2,3,1,0:T(8,128)}), f32[32,32,32,16]{2,3,1,0:T(8,128)}) %all-gather.2.cloned.1.call-update) | async-done | bytes 2097168 | tf_op jit(solution)/shard_map/all_gather | solution.py:45
  71.9 4.0 %reduce_sum.51 = f32[32,32,16]{1,2,0:T(8,128)S(1)} reduce(f32[32,32,32,16]{2,3,1,0:T(8,128)} %all-gather.2.cloned.1.call-done, f32[]{:T(128)} %constant.25.clone.1), dimensions={0}, to_apply=%region_5.6 | reduce | flops 507904 | bytes 2162692 | tf_op jit(solution)/shard_map/reduce_sum | solution.py:45
  76.0 0.0 copy-start.1
  76.0 0.0 copy-start.2
  76.0 0.7 convert_reduce_fusion
  76.7 0.1 convert_element_type.48
  76.8 0.0 copy-start.5
  76.8 2.6 %convolution_convert_fusion.1 = bf16[512,1024]{1,0:T(8,128)(2,1)} fusion(bf16[256,1024]{1,0:T(8,128)(2,1)} %fusion.3, s32[512]{0:T(512)S(1)} %convert_element_type.48), kind=kOutput, calls=%fused_computation.3 | convolution fusion | flops 269090816 | bytes 1574912 | tf_op jit(solution)/shard_map/dot_general | solution.py:56
  79.4 5.5 %all-to-all-start = ((bf16[32,16,1024]{2,1,0:T(8,128)(2,1)}), bf16[32,16,1024]{2,1,0:T(8,128)(2,1)}, u32[]{:S(2)}, u32[]{:S(2)}) async-start(bf16[32,16,1024]{2,1,0:T(8,128)(2,1)} %bitcast.6), calls=%async_computation | async-start | bytes 2097152 | tf_op jit(solution)/shard_map/all_to_all | solution.py:61
  84.9 0.0 copy-done.1
  85.0 0.0 copy-done.2
  85.0 4.3 %select_reduce_fusion = bf16[256,512]{1,0:T(8,128)(2,1)S(1)} fusion(f32[256,50]{0,1:T(8,128)S(1)} %broadcast_divide_fusion, s32[256,50]{0,1:T(8,128)S(1)} %copy-done.2), kind=kLoop, calls=%fused_computation | loop fusion | flops 19529728 | bytes 364544 | tf_op jit(solution)/shard_map/reduce_sum | solution.py:52
  89.4 12.5 %all-to-all-done = bf16[32,16,1024]{2,1,0:T(8,128)(2,1)} async-done(((bf16[32,16,1024]{2,1,0:T(8,128)(2,1)}), bf16[32,16,1024]{2,1,0:T(8,128)(2,1)}, u32[]{:S(2)}, u32[]{:S(2)}) %all-to-all-start) | async-done | bytes 1048608 | tf_op jit(solution)/shard_map/all_to_all | solution.py:61
  101.9 0.0 copy-done
  101.9 0.0 copy-done.5
  101.9 3.3 %multiply_reduce_fusion = (f32[256]{0:T(256)S(1)}, f32[256,1024]{1,0:T(8,128)}) fusion(f32[1024]{0:T(1024)S(1)} %copy-done.5, f32[256,1024]{1,0:T(8,128)S(1)} %fusion.13, bf16[1024,1024]{1,0:T(8,128)(2,1)S(1)} %copy-done, bf16[512,1024]{1,0:T(8,128)(2,1)} %bitcast.7, bf16[256,512]{1,0:T(8,128)(2,1)S(1)} %select_reduce_fusion), kind=kOutput, calls=%fused_computation.14 | convolution fusion | flops 806878976 | bytes 5510144 | tf_op jit(solution)/shard_map/dot_general | solution.py:71
  105.2 0.0 copy-start.4
  105.2 1.8 %convolution_convert_fusion = bf16[512,1024]{1,0:T(8,128)(2,1)S(1)} fusion(f32[256,1024]{1,0:T(8,128)} %get-tuple-element.6, f32[256]{0:T(256)S(1)} %add_rsqrt_fusion, s32[256]{0:T(256)S(1)} %bitcast.44), kind=kOutput, calls=%fused_computation.2 | convolution fusion | flops 269615104 | bytes 2099200 | tf_op jit(solution)/shard_map/dot_general | solution.py:79
  107.0 20.6 %all_to_all.15 = bf16[32,16,1024]{2,1,0:T(8,128)(2,1)S(1)} all-to-all(bf16[32,16,1024]{2,1,0:T(8,128)(2,1)S(1)} %bitcast.38), channel_id=1, replica_groups=mesh['graph'=8,'index'=32] {'index'}, dimensions={0} | all-to-all | bytes 2097152 | tf_op jit(solution)/shard_map/all_to_all | solution.py:83
  127.7 0.0 copy-done.4
  127.7 0.5 convolution_convert_fusion.3
  128.1 12.7 %all_to_all.16 = bf16[32,16,256]{2,1,0:T(8,128)(2,1)S(1)} all-to-all(bf16[32,16,256]{2,1,0:T(8,128)(2,1)S(1)} %bitcast.41), channel_id=1, replica_groups=mesh['graph'=8,'index'=32] {'index'}, dimensions={0} | all-to-all | bytes 524288 | tf_op jit(solution)/shard_map/all_to_all | solution.py:88
  140.8 0.9 convolution_convert_fusion.4
  (8 shorter events, 0.1 us)
Async XLA Ops:
  6.5 95.3 %copy-start = (bf16[1024,1024]{1,0:T(8,128)(2,1)S(1)}, bf16[1024,1024]{1,0:T(8,128)(2,1)}, u32[]{:S(2)}) copy-start(bf16[1024,1024]{1,0:T(8,128)(2,1)} %param.15) | copy-start | bytes 6291460
  6.5 65.4 %all-gather.2.cloned.1.call-start = ((), (), s32[]{:S(2)}) async-start(), calls=%async_computation.3 | async-start | bytes 8650752 | tf_op jit(solution)/shard_map/all_gather | solution.py:45
  8.2 3.3 %copy-start.3 = (s32[256,1]{0,1:T(1,128)S(1)}, s32[256,1]{0,1:T(1,128)}, u32[]{:S(2)}) copy-start(s32[256,1]{0,1:T(1,128)} %param.21) | copy-start | bytes 3076
  76.0 9.0 %copy-start.1 = (f32[256,50]{0,1:T(8,128)S(1)}, f32[256,50]{0,1:T(8,128)}, u32[]{:S(2)}) copy-start(f32[256,50]{0,1:T(8,128)} %param.20) | copy-start | bytes 153604
  76.0 9.0 %copy-start.2 = (s32[256,50]{0,1:T(8,128)S(1)}, s32[256,50]{0,1:T(8,128)}, u32[]{:S(2)}) copy-start(s32[256,50]{0,1:T(8,128)} %param.19) | copy-start | bytes 153604
  76.8 25.1 %copy-start.5 = (f32[1024]{0:T(1024)S(1)}, f32[1024]{0:T(1024)}, u32[]{:S(2)}) copy-start(f32[1024]{0:T(1024)} %param.16) | copy-start | bytes 12292
  79.4 22.5 %all-to-all-start = ((bf16[32,16,1024]{2,1,0:T(8,128)(2,1)}), bf16[32,16,1024]{2,1,0:T(8,128)(2,1)}, u32[]{:S(2)}, u32[]{:S(2)}) async-start(bf16[32,16,1024]{2,1,0:T(8,128)(2,1)} %bitcast.6), calls=%async_computation | async-start | bytes 2097152 | tf_op jit(solution)/shard_map/all_to_all | solution.py:61
  105.2 22.5 %copy-start.4 = (bf16[256,1024]{1,0:T(8,128)(2,1)S(1)}, bf16[256,1024]{1,0:T(8,128)(2,1)}, u32[]{:S(2)}) copy-start(bf16[256,1024]{1,0:T(8,128)(2,1)} %param.17) | copy-start | bytes 1572868
Sparse Core Ops, SparseCore 0:
  9.9 61.9 all-gather.1
